TPU v7x, 512 devices: a whole 4x4x16 slice. The times are simulated.
512 devices in a mesh: ctx: 32 (over z_hi, x, y), exp: 16 (over z_lo, core).
Axes of the slice: x: 4, y: 4, z: 16 (z_hi: 2, z_lo: 8; z = z_hi * 8 + z_lo), core: 2. Of those that a mesh axis runs over, the one named last changes fastest.
Arguments:
- residual: bfloat16 [4096, 4096], P(('ctx', 'exp')), may hold values from -6 to 6
- queries: bfloat16 [4096, 4096], P('ctx', 'exp'), may hold values from -8 to 8
- keys: bfloat16 [4096, 256], P('ctx'), may hold values from -8 to 8
- values: bfloat16 [4096, 256], P('ctx'), may hold values from -6 to 6
- span_pos: int32 [64], replicated, may hold values from 0 to 63, each once
- out_proj: bfloat16 [4096, 4096], P('exp'), may hold values from -0.71875 to 0.71875
- norm_gain: float32 [4096], replicated, may hold values from 0.25 to 1.75
- expert_gate: bfloat16 [16, 4096, 768], P('exp', None, 'ctx'), may hold values from -0.09375 to 0.09375
- expert_up: bfloat16 [16, 4096, 768], P('exp', None, 'ctx'), may hold values from -0.09375 to 0.09375
- expert_ids: int32 [4096, 8], P(('ctx', 'exp')), may hold values from 0 to 15, all different within a row; in each aligned block of 8 rows (0 to 7, 8 to 15, ...) at most 6 rows name the same one
- route_weight: float32 [4096, 8], P(('ctx', 'exp')), may hold values from 0.25 to 2
Outputs:
- mixed: bfloat16 [4096, 4096], P(('ctx', 'exp'))
- routed: bfloat16 [4096, 8, 768], P(('ctx', 'exp'))
Inputs may be any that keep to these rules, and one draw needn't show every extreme that they name: `span_pos`: every span number appears once. `expert_ids`: each row names 8 different experts; among the rows of one device (8 rows in a row, aligned) no expert is named more than 6 times, and in some device's rows some expert is named exactly 6 times.
All inputs are finite; a program needn't handle non-finite values.
Results may differ from a plain program's by a relative error of at most 0.035.
Values may be sent and summed in bfloat16 or wider, within the bound.
No kernel may reach another device: no remote copies, remote signals or barrier semaphores. Data moves between devices by JAX's collectives and lax.ppermute only.
A program may use at most 128 MiB of HBM per device.

v0:
```python
import math
import jax
import jax.numpy as jnp
import numpy as np
from jax import lax
from jax.sharding import Mesh
from jax.sharding import PartitionSpec as P

D = 4096
HQ = 32
KVH = 2
HD = 128
FE = 768
EXPERTS = 16
TOPK = 8
CH = 64
CTX = ("zh", "x", "y")
EXP = ("zl", "c")


def stored_positions(span_pos, rows):
    span = rows // CH
    table = span[:, None] == jnp.arange(span_pos.shape[0], dtype=jnp.int32)[None, :]
    base = jnp.sum(jnp.where(table, span_pos[None, :], 0), axis=1)
    return base * CH + rows % CH


def doubling_bits(n):
    bits = []
    b = n // 2
    while b >= 1:
        bits.append(b)
        b //= 2
    return bits


def gather_by_doubling(piece, n):
    idx = lax.axis_index(CTX)
    cur = piece
    order = [0]
    for bit in doubling_bits(n):
        other = lax.ppermute(cur, CTX, [(i, i ^ bit) for i in range(n)])
        low = idx & bit == 0
        cur = jnp.where(low, jnp.concatenate([cur, other]), jnp.concatenate([other, cur]))
        order = order + [o + bit for o in order]
    return (cur, order)


def shards(
    residual,
    queries,
    keys,
    values,
    span_pos,
    out_proj,
    norm_gain,
    expert_gate,
    expert_up,
    expert_ids,
    route_weight,
    n_ctx,
    n_xy,
    n_zh,
):
    tok_rows = queries.shape[0]
    per_device = queries.shape[1] // HD
    group = HQ // KVH
    ctx_index = lax.axis_index(CTX)
    exp_index = lax.axis_index(EXP)
    n_exp = EXPERTS
    fe_dev = expert_gate.shape[2]
    w_local = jnp.concatenate([expert_gate[0].T, expert_up[0].T], axis=0)
    zh_index = lax.axis_index("zh")
    core_index = lax.axis_index("c")
    kv_head = exp_index * per_device // group
    own_keys = lax.dynamic_slice_in_dim(keys, kv_head * HD, HD, 1)
    own_values = lax.dynamic_slice_in_dim(values, kv_head * HD, HD, 1)
    kv_local = jnp.where(core_index == 0, own_keys, own_values)
    bits = doubling_bits(n_ctx)
    first = bits[0]
    kv_other = lax.ppermute(kv_local, CTX, [(i, i ^ first) for i in range(n_ctx)])
    w_other = lax.ppermute(w_local, "zh", [(0, 1), (1, 0)])
    w_pair = jnp.where(
        zh_index == 0, jnp.concatenate([w_local, w_other]), jnp.concatenate([w_other, w_local])
    )
    w_all = lax.all_gather(w_pair, ("x", "y"), axis=0, tiled=True)
    low = ctx_index & first == 0
    cur = jnp.where(
        low, jnp.concatenate([kv_local, kv_other]), jnp.concatenate([kv_other, kv_local])
    )
    order = [0, first]
    for bit in bits[1:]:
        other = lax.ppermute(cur, CTX, [(i, i ^ bit) for i in range(n_ctx)])
        low = ctx_index & bit == 0
        cur = jnp.where(low, jnp.concatenate([cur, other]), jnp.concatenate([other, cur]))
        order = order + [o + bit for o in order]
    partner = lax.ppermute(cur, "c", [(0, 1), (1, 0)])
    key_piece = jnp.where(core_index == 0, cur, partner)
    value_piece = jnp.where(core_index == 0, partner, cur)
    length = key_piece.shape[0]
    block_ctx = jnp.asarray(np.array(order, np.int32))
    key_rows_all = jnp.repeat(block_ctx, tok_rows) * tok_rows + jnp.tile(
        jnp.arange(tok_rows, dtype=jnp.int32), n_ctx
    )
    query_pos = stored_positions(
        span_pos, ctx_index * tok_rows + jnp.arange(tok_rows, dtype=jnp.int32)
    )
    query_heads = queries.reshape(tok_rows, per_device, HD)
    scale = 1.0 / math.sqrt(HD)
    carry = (
        jnp.full((per_device, tok_rows), -1e30, jnp.float32),
        jnp.zeros((per_device, tok_rows), jnp.float32),
        jnp.zeros((per_device, tok_rows, HD), jnp.float32),
    )
    block = min(length, 1024)
    for begin in range(0, length, block):
        stop = min(begin + block, length)
        attend_key_piece = key_piece[begin:stop]
        attend_value_piece = value_piece[begin:stop]
        attend_running, attend_total, attend_accum = carry
        key_pos = stored_positions(span_pos, key_rows_all[begin:stop])
        scores = (
            jnp.einsum(
                "tqd,nd->qtn", query_heads, attend_key_piece, preferred_element_type=jnp.float32
            )
            * scale
        )
        visible = key_pos[None, None, :] <= query_pos[None, :, None]
        block_top = jnp.max(jnp.where(visible, scores, -1e30), axis=2)
        new_top = jnp.maximum(attend_running, block_top)
        factor = jnp.exp(attend_running - new_top)
        probs = jnp.where(visible, jnp.exp(scores - new_top[:, :, None]), 0.0)
        attend_total = attend_total * factor + jnp.sum(probs, axis=2)
        summed = jnp.einsum(
            "qtn,nd->qtd",
            probs.astype(jnp.bfloat16),
            attend_value_piece,
            preferred_element_type=jnp.float32,
        )
        attend_accum = attend_accum * factor[:, :, None] + summed
        carry = (new_top, attend_total, attend_accum)
    running, total, accum = carry
    attn = (accum / total[:, :, None]).astype(jnp.bfloat16)
    attn = jnp.transpose(attn, (1, 0, 2)).reshape(tok_rows, per_device * HD)
    tok_dev = residual.shape[0]
    share = jnp.dot(attn, out_proj, preferred_element_type=jnp.float32).astype(jnp.bfloat16)
    zl_index = lax.axis_index("zl")
    n_zl = n_exp // 2
    by_core = jnp.transpose(share.reshape(n_zl, 2, tok_dev, D), (1, 0, 2, 3))
    keep = jnp.where(core_index == 0, by_core[0], by_core[1])
    give = jnp.where(core_index == 0, by_core[1], by_core[0])
    got = lax.ppermute(give, "c", [(0, 1), (1, 0)])
    part = keep.astype(jnp.float32) + got.astype(jnp.float32)
    pair_sum = part.astype(jnp.bfloat16)
    shares = lax.all_to_all(pair_sum, "zl", split_axis=0, concat_axis=0, tiled=True)
    head_total = jnp.sum(shares.astype(jnp.float32), axis=0)
    mixed = (residual.astype(jnp.float32) + head_total).astype(jnp.bfloat16)
    mixed_f = mixed.astype(jnp.float32)
    square = jnp.mean(mixed_f * mixed_f, axis=1, keepdims=True)
    normed = (mixed_f * lax.rsqrt(square + 1e-06) * norm_gain[None, :]).astype(jnp.bfloat16)
    ids_rw = jnp.concatenate([expert_ids.astype(jnp.float32), route_weight], axis=1)
    ids_rw_all = lax.all_to_all(
        jnp.broadcast_to(ids_rw[None], (n_exp,) + ids_rw.shape),
        EXP,
        split_axis=0,
        concat_axis=0,
        tiled=True,
    ).reshape(n_exp * tok_dev, 2 * TOPK)
    ids_all = ids_rw_all[:, :TOPK].astype(jnp.int32)
    rw_all = ids_rw_all[:, TOPK:]
    cur = normed
    order = [0]
    for bit in doubling_bits(n_zl):
        other = lax.ppermute(cur, "zl", [(i, i ^ bit) for i in range(n_zl)])
        low = zl_index & bit == 0
        cur = jnp.where(low, jnp.concatenate([cur, other]), jnp.concatenate([other, cur]))
        order = order + [o + bit for o in order]
    partner = lax.ppermute(cur, "c", [(0, 1), (1, 0)])
    both = jnp.where(
        core_index == 0, jnp.concatenate([cur, partner]), jnp.concatenate([partner, cur])
    )
    blocks = []
    for src in range(n_exp):
        q = src % 2 * n_zl + order.index(src // 2)
        blocks.append(both[q * tok_dev : (q + 1) * tok_dev])
    gathered = jnp.concatenate(blocks)
    normed_all = gathered
    most_slots = tok_dev
    chosen = jnp.any(ids_all == exp_index, axis=1).astype(jnp.int32).reshape(n_exp, tok_dev)
    rank = jnp.cumsum(chosen, axis=1) - chosen
    dest = jnp.where(
        chosen == 1, jnp.arange(n_exp, dtype=jnp.int32)[:, None] * most_slots + rank, -1
    ).reshape(-1)
    slot_of = jnp.arange(n_exp * most_slots, dtype=jnp.int32)[:, None] == dest[None, :]
    placing = slot_of.astype(jnp.bfloat16)
    rw_tok = jnp.sum(jnp.where(ids_all == exp_index, rw_all, 0.0), axis=1)
    rw_slot = jnp.sum(jnp.where(slot_of, rw_tok[None, :], 0.0), axis=1)
    received = jnp.dot(placing, normed_all, preferred_element_type=jnp.float32).astype(jnp.bfloat16)
    received = lax.optimization_barrier(received)
    ids_flat = expert_ids.reshape(-1)
    onehot = (ids_flat[:, None] == jnp.arange(EXPERTS, dtype=jnp.int32)[None, :]).astype(jnp.int32)
    earlier = jnp.cumsum(onehot, axis=0) - onehot
    slot = jnp.sum(earlier * onehot, axis=1)
    target = ids_flat * most_slots + slot
    proj = jnp.einsum("fd,sd->fs", w_all, received, preferred_element_type=jnp.float32)
    proj = proj.reshape(n_xy, n_zh, 2, fe_dev, EXPERTS * most_slots)
    hidden = jax.nn.silu(proj[:, :, 0]) * proj[:, :, 1]
    hidden = jnp.transpose(hidden, (1, 0, 2, 3)).reshape(FE, EXPERTS * most_slots)
    hidden = (hidden * rw_slot[None, :]).astype(jnp.bfloat16).T.reshape(EXPERTS, most_slots, FE)
    returned = lax.all_to_all(hidden, EXP, split_axis=0, concat_axis=0, tiled=True).reshape(
        EXPERTS * most_slots, FE
    )
    routed = jnp.take(returned, target, axis=0)
    return (mixed, routed.reshape(tok_dev, TOPK, FE))


def solution(mesh):
    n_ctx = mesh.shape["ctx"]
    n_exp = mesh.shape["exp"]
    n_zh = 2
    n_xy = n_ctx // n_zh
    side = int(round(math.sqrt(n_xy)))
    n_zl = n_exp // 2
    fine = Mesh(mesh.devices.reshape(n_zh, side, n_xy // side, n_zl, 2), CTX + EXP)
    tok = CTX + EXP
    in_specs = (
        P(tok, None),
        P(CTX, EXP),
        P(CTX, None),
        P(CTX, None),
        P(),
        P(EXP, None),
        P(),
        P(EXP, None, CTX),
        P(EXP, None, CTX),
        P(tok, None),
        P(tok, None),
    )
    out_specs = (P(tok, None), P(tok, None, None))

    def body(*args):
        return shards(*args, n_ctx=n_ctx, n_xy=n_xy, n_zh=n_zh)

    return jax.shard_map(body, mesh=fine, in_specs=in_specs, out_specs=out_specs, check_vma=False)
```

profile of v0, /device:TPU:1, one launch (start us, length us, event | category | flops | bytes accessed | tf_op | source)
XLA Modules:
  0.0 239.2 jit_solution(13024758327320912529)
XLA Ops:
  7.3 0.9 dynamic-slice_select_fusion
  8.2 16.3 %collective-permute-start = (bf16[128,128]{1,0:T(8,128)(2,1)S(1)}, bf16[128,128]{1,0:T(8,128)(2,1)S(1)}, u32[]{:S(2)}, u32[]{:S(2)}) collective-permute-start(bf16[128,128]{1,0:T(8,128)(2,1)S(1)} %dynamic-slice_select_fusion), channel_id=1, source_target_pairs={{0,256},{16,272},{32,288},{48,304},{64,320},{80,336},{96,352},{112... | collective-permute-start | bytes 98312 | tf_op jit(solution)/shard_map/ppermute | solution.py:81
  24.5 1.4 collective-permute-done
  25.9 4.7 %collective-permute-start.1 = (bf16[256,128]{1,0:T(8,128)(2,1)S(1)}, bf16[256,128]{1,0:T(8,128)(2,1)S(1)}, u32[]{:S(2)}, u32[]{:S(2)}) collective-permute-start(bf16[256,128]{1,0:T(8,128)(2,1)S(1)} %maximum_select_fusion.9), channel_id=1, source_target_pairs={{0,128},{16,144},{32,160},{48,176},{64,192},{80,208},{96,224},{112... | collective-permute-start | bytes 196616 | tf_op jit(solution)/shard_map/ppermute | solution.py:93
  30.5 1.8 collective-permute-done.1
  32.4 3.1 %collective-permute-start.2 = (bf16[512,128]{1,0:T(8,128)(2,1)S(1)}, bf16[512,128]{1,0:T(8,128)(2,1)S(1)}, u32[]{:S(2)}, u32[]{:S(2)}) collective-permute-start(bf16[512,128]{1,0:T(8,128)(2,1)S(1)} %maximum_select_fusion.7), channel_id=1, source_target_pairs={{0,64},{16,80},{32,96},{48,112},{64,0},{80,16},{96,32},{112,48},{1... | collective-permute-start | bytes 393224 | tf_op jit(solution)/shard_map/ppermute | solution.py:93
  35.6 2.6 %collective-permute-done.2 = bf16[512,128]{1,0:T(8,128)(2,1)S(1)} collective-permute-done((bf16[512,128]{1,0:T(8,128)(2,1)S(1)}, bf16[512,128]{1,0:T(8,128)(2,1)S(1)}, u32[]{:S(2)}, u32[]{:S(2)}) %collective-permute-start.2) | collective-permute-done | bytes 131104 | tf_op jit(solution)/shard_map/ppermute | solution.py:93
  38.2 4.8 %collective-permute-start.3 = (bf16[1024,128]{1,0:T(8,128)(2,1)S(1)}, bf16[1024,128]{1,0:T(8,128)(2,1)S(1)}, u32[]{:S(2)}, u32[]{:S(2)}) collective-permute-start(bf16[1024,128]{1,0:T(8,128)(2,1)S(1)} %maximum_select_fusion.5), channel_id=1, source_target_pairs={{0,32},{16,48},{32,0},{48,16},{64,96},{80,112},{96,64},{112,80},{1... | collective-permute-start | bytes 786440 | tf_op jit(solution)/shard_map/ppermute | solution.py:93
  43.1 1.8 pad_maximum_fusion
  44.9 12.5 %collective-permute-start.7 = (bf16[48,4096]{1,0:T(8,128)(2,1)}, bf16[48,4096]{1,0:T(8,128)(2,1)}, u32[]{:S(2)}, u32[]{:S(2)}) collective-permute-start(bf16[48,4096]{1,0:T(8,128)(2,1)} %pad_maximum_fusion), channel_id=1, source_target_pairs={{0,256},{256,0},{1,257},{257,1},{2,258},{258,2},{3,259},{259,3},{4... | collective-permute-start | bytes 1179656 | tf_op jit(solution)/shard_map/ppermute | solution.py:82
  57.4 0.7 iota_add_fusion
  58.2 2.3 collective-permute-start.4
  60.9 8.4 %collective-permute-done.4 = bf16[2048,128]{1,0:T(8,128)(2,1)S(1)} collective-permute-done((bf16[2048,128]{1,0:T(8,128)(2,1)S(1)}, bf16[2048,128]{1,0:T(8,128)(2,1)S(1)}, u32[]{:S(2)}, u32[]{:S(2)}) %collective-permute-start.4) | collective-permute-done | bytes 524320 | tf_op jit(solution)/shard_map/ppermute | solution.py:93
  69.5 7.2 %collective-permute-start.5 = (bf16[4096,128]{1,0:T(8,128)(2,1)S(1)}, bf16[4096,128]{1,0:T(8,128)(2,1)}, u32[]{:S(2)}, u32[]{:S(2)}) collective-permute-start(bf16[4096,128]{1,0:T(8,128)(2,1)S(1)} %maximum_select_fusion), channel_id=1, source_target_pairs={{0,1},{1,0},{2,3},{3,2},{4,5},{5,4},{6,7},{7,6},{8,9},{9,8},{10,11... | collective-permute-start | bytes 3145736 | tf_op jit(solution)/shard_map/ppermute | solution.py:97
  76.7 0.5 and_select_fusion.1
  77.2 0.8 select_reduce_fusion.10
  78.0 1.9 broadcast_compare_fusion.1
  79.9 2.2 maximum_select_fusion.2
  82.2 1.6 broadcast_select_fusion
  85.4 0.4 fusion.14
  85.8 0.4 fusion.18
  86.2 0.4 fusion.11
  86.6 0.4 fusion.9
  87.0 0.4 fusion.7
  87.3 0.4 fusion.12
  87.7 0.5 convolution_convert_fusion.1
  88.3 12.6 %collective-permute-start.6 = (bf16[8,8,4096]{2,1,0:T(8,128)(2,1)S(1)}, bf16[8,8,4096]{2,1,0:T(8,128)(2,1)S(1)}, u32[]{:S(2)}, u32[]{:S(2)}) collective-permute-start(bf16[8,8,4096]{2,1,0:T(8,128)(2,1)S(1)} %fusion.26), channel_id=1, source_target_pairs={{0,1},{1,0},{2,3},{3,2},{4,5},{5,4},{6,7},{7,6},{8,9},{9,8},{10,11... | collective-permute-start | bytes 1572872 | tf_op jit(solution)/shard_map/ppermute | solution.py:152
  100.9 1.5 collective-permute-done.6
  102.6 34.0 %all_to_all.15 = bf16[8,8,4096]{2,1,0:T(8,128)(2,1)S(1)} all-to-all(bf16[8,8,4096]{2,1,0:T(8,128)(2,1)S(1)} %fusion.13), channel_id=1, replica_groups=mesh['zh'=2,'x'=4,'y'=4,'zl'=8,'c'=2] {'zl'}, dimensions={0} | all-to-all | bytes 1048576 | tf_op jit(solution)/shard_map/all_to_all | solution.py:155
  137.0 4.6 %collective-permute-start.8 = (bf16[8,4096]{1,0:T(8,128)(2,1)S(1)}, bf16[8,4096]{1,0:T(8,128)(2,1)S(1)}, u32[]{:S(2)}, u32[]{:S(2)}) collective-permute-start(bf16[8,4096]{1,0:T(8,128)(2,1)S(1)} %fusion.44), channel_id=1, source_target_pairs={{0,8},{2,10},{4,12},{6,14},{8,0},{10,2},{12,4},{14,6},{1,9},{3,11}... | collective-permute-start | bytes 196616 | tf_op jit(solution)/shard_map/ppermute | solution.py:174
  141.6 4.3 %collective-permute-done.8 = bf16[8,4096]{1,0:T(8,128)(2,1)S(1)} collective-permute-done((bf16[8,4096]{1,0:T(8,128)(2,1)S(1)}, bf16[8,4096]{1,0:T(8,128)(2,1)S(1)}, u32[]{:S(2)}, u32[]{:S(2)}) %collective-permute-start.8) | collective-permute-done | bytes 65568 | tf_op jit(solution)/shard_map/ppermute | solution.py:174
  146.0 3.6 %collective-permute-start.9 = (bf16[16,4096]{1,0:T(8,128)(2,1)S(1)}, bf16[16,4096]{1,0:T(8,128)(2,1)S(1)}, u32[]{:S(2)}, u32[]{:S(2)}) collective-permute-start(bf16[16,4096]{1,0:T(8,128)(2,1)S(1)} %maximum_select_fusion.8), channel_id=1, source_target_pairs={{0,4},{2,6},{4,0},{6,2},{8,12},{10,14},{12,8},{14,10},{1,5},{3,7},... | collective-permute-start | bytes 393224 | tf_op jit(solution)/shard_map/ppermute | solution.py:174
  149.7 0.7 reshape.398
  150.4 10.6 %all-to-all-start.1 = ((f32[16,1,128]{2,1,0:T(1,128)}), f32[16,1,128]{2,1,0:T(1,128)S(1)}, u32[]{:S(2)}, u32[]{:S(2)}) async-start(f32[16,1,128]{2,1,0:T(1,128)} %reshape.398), calls=%async_computation.1 | async-start | bytes 16384 | tf_op jit(solution)/shard_map/all_to_all | solution.py:162
  161.0 3.3 %collective-permute-start.10 = (bf16[32,4096]{1,0:T(8,128)(2,1)S(1)}, bf16[32,4096]{1,0:T(8,128)(2,1)S(1)}, u32[]{:S(2)}, u32[]{:S(2)}) collective-permute-start(bf16[32,4096]{1,0:T(8,128)(2,1)S(1)} %maximum_select_fusion.6), channel_id=1, source_target_pairs={{0,2},{2,0},{4,6},{6,4},{8,10},{10,8},{12,14},{14,12},{1,3},{3,1},... | collective-permute-start | bytes 786440 | tf_op jit(solution)/shard_map/ppermute | solution.py:174
  164.6 6.1 %all-to-all-done.1 = f32[16,1,128]{2,1,0:T(1,128)S(1)} async-done(((f32[16,1,128]{2,1,0:T(1,128)}), f32[16,1,128]{2,1,0:T(1,128)S(1)}, u32[]{:S(2)}, u32[]{:S(2)}) %all-to-all-start.1) | async-done | bytes 8224 | tf_op jit(solution)/shard_map/all_to_all | solution.py:162
  170.7 0.5 broadcast.430
  171.2 0.7 reduce
  172.3 2.6 %collective-permute-start.11 = (bf16[64,4096]{1,0:T(8,128)(2,1)S(1)}, bf16[64,4096]{1,0:T(8,128)(2,1)S(1)}, u32[]{:S(2)}, u32[]{:S(2)}) collective-permute-start(bf16[64,4096]{1,0:T(8,128)(2,1)S(1)} %maximum_select_fusion.4), channel_id=1, source_target_pairs={{0,1},{1,0},{2,3},{3,2},{4,5},{5,4},{6,7},{7,6},{8,9},{9,8},{10,11... | collective-permute-start | bytes 1572872 | tf_op jit(solution)/shard_map/ppermute | solution.py:178
  175.4 1.0 collective-permute-done.11
  176.9 0.4 convolution_convert_fusion
  177.3 20.8 %all-gather.2.cloned.1.call-done = bf16[1536,4096]{1,0:T(8,128)(2,1)} async-done(((bf16[96,4096]{1,0:T(8,128)(2,1)}), bf16[1536,4096]{1,0:T(8,128)(2,1)}) %all-gather.2.cloned.1.call-update) | async-done | bytes 12582928 | tf_op jit(solution)/shard_map/all_gather | solution.py:86
  198.1 6.4 %fusion.94 = f32[1536,128]{1,0:T(8,128)S(1)} fusion(bf16[1536,4096]{1,0:T(8,128)(2,1)} %all-gather.2.cloned.1.call-done, bf16[128,4096]{1,0:T(8,128)(2,1)S(1)} %convolution_convert_fusion), kind=kOutput, calls=%fused_computation.228 | convolution fusion | flops 1610612736 | bytes 14417920 | tf_op jit(solution)/shard_map/fd,sd->fs/dot_general | solution.py:205
  204.8 0.8 copy.132
  205.6 10.7 %all-to-all-start.2 = ((bf16[16,8,768]{2,1,0:T(8,128)(2,1)}), bf16[16,8,768]{2,1,0:T(8,128)(2,1)S(1)}, u32[]{:S(2)}, u32[]{:S(2)}) async-start(bf16[16,8,768]{2,1,0:T(8,128)(2,1)} %bitcast.50), calls=%async_computation.2 | async-start | bytes 393216 | tf_op jit(solution)/shard_map/all_to_all | solution.py:210
  216.8 14.1 %all-to-all-done.2 = bf16[16,8,768]{2,1,0:T(8,128)(2,1)S(1)} async-done(((bf16[16,8,768]{2,1,0:T(8,128)(2,1)}), bf16[16,8,768]{2,1,0:T(8,128)(2,1)S(1)}, u32[]{:S(2)}, u32[]{:S(2)}) %all-to-all-start.2) | async-done | bytes 196640 | tf_op jit(solution)/shard_map/all_to_all | solution.py:210
  230.9 0.7 gather_fusion
  231.6 0.7 bitcast_select_fusion.2
  (106 shorter events, 5.4 us)
Async XLA Ops:
  7.2 80.6 %copy-start = (bf16[256,4096]{1,0:T(8,128)(2,1)S(1)}, bf16[256,4096]{1,0:T(8,128)(2,1)}, u32[]{:S(2)}) copy-start(bf16[256,4096]{1,0:T(8,128)(2,1)} %param.17) | copy-start | bytes 6291460
  7.2 53.4 %copy-start.12 = (s32[64]{0:T(128)S(1)}, s32[64]{0:T(128)}, u32[]{:S(2)}) copy-start(s32[64]{0:T(128)} %param.16) | copy-start | bytes 772
  7.2 190.9 %all-gather.2.cloned.1.call-start = ((), (), s32[]{:S(2)}) async-start(), calls=%async_computation.3 | async-start | bytes 13369344 | tf_op jit(solution)/shard_map/all_gather | solution.py:86
  8.2 17.7 %collective-permute-start = (bf16[128,128]{1,0:T(8,128)(2,1)S(1)}, bf16[128,128]{1,0:T(8,128)(2,1)S(1)}, u32[]{:S(2)}, u32[]{:S(2)}) collective-permute-start(bf16[128,128]{1,0:T(8,128)(2,1)S(1)} %dynamic-slice_select_fusion), channel_id=1, source_target_pairs={{0,256},{16,272},{32,288},{48,304},{64,320},{80,336},{96,352},{112... | collective-permute-start | bytes 98312 | tf_op jit(solution)/shard_map/ppermute | solution.py:81
  25.9 6.5 %collective-permute-start.1 = (bf16[256,128]{1,0:T(8,128)(2,1)S(1)}, bf16[256,128]{1,0:T(8,128)(2,1)S(1)}, u32[]{:S(2)}, u32[]{:S(2)}) collective-permute-start(bf16[256,128]{1,0:T(8,128)(2,1)S(1)} %maximum_select_fusion.9), channel_id=1, source_target_pairs={{0,128},{16,144},{32,160},{48,176},{64,192},{80,208},{96,224},{112... | collective-permute-start | bytes 196616 | tf_op jit(solution)/shard_map/ppermute | solution.py:93
  32.4 5.7 %collective-permute-start.2 = (bf16[512,128]{1,0:T(8,128)(2,1)S(1)}, bf16[512,128]{1,0:T(8,128)(2,1)S(1)}, u32[]{:S(2)}, u32[]{:S(2)}) collective-permute-start(bf16[512,128]{1,0:T(8,128)(2,1)S(1)} %maximum_select_fusion.7), channel_id=1, source_target_pairs={{0,64},{16,80},{32,96},{48,112},{64,0},{80,16},{96,32},{112,48},{1... | collective-permute-start | bytes 393224 | tf_op jit(solution)/shard_map/ppermute | solution.py:93
  38.2 19.9 %collective-permute-start.3 = (bf16[1024,128]{1,0:T(8,128)(2,1)S(1)}, bf16[1024,128]{1,0:T(8,128)(2,1)S(1)}, u32[]{:S(2)}, u32[]{:S(2)}) collective-permute-start(bf16[1024,128]{1,0:T(8,128)(2,1)S(1)} %maximum_select_fusion.5), channel_id=1, source_target_pairs={{0,32},{16,48},{32,0},{48,16},{64,96},{80,112},{96,64},{112,80},{1... | collective-permute-start | bytes 786440 | tf_op jit(solution)/shard_map/ppermute | solution.py:93
  44.9 35.0 %copy-start.1 = (bf16[1,4096,24]{1,2,0:T(8,128)(2,1)S(1)}, bf16[1,4096,24]{1,2,0:T(8,128)(2,1)}, u32[]{:S(2)}) copy-start(bf16[1,4096,24]{1,2,0:T(8,128)(2,1)} %param.20) | copy-start | bytes 589828
  44.9 35.0 %copy-start.2 = (bf16[1,4096,24]{1,2,0:T(8,128)(2,1)S(1)}, bf16[1,4096,24]{1,2,0:T(8,128)(2,1)}, u32[]{:S(2)}) copy-start(bf16[1,4096,24]{1,2,0:T(8,128)(2,1)} %param.19) | copy-start | bytes 589828
  44.9 35.0 %collective-permute-start.7 = (bf16[48,4096]{1,0:T(8,128)(2,1)}, bf16[48,4096]{1,0:T(8,128)(2,1)}, u32[]{:S(2)}, u32[]{:S(2)}) collective-permute-start(bf16[48,4096]{1,0:T(8,128)(2,1)} %pad_maximum_fusion), channel_id=1, source_target_pairs={{0,256},{256,0},{1,257},{257,1},{2,258},{258,2},{3,259},{259,3},{4... | collective-permute-start | bytes 1179656 | tf_op jit(solution)/shard_map/ppermute | solution.py:82
  58.2 11.0 %collective-permute-start.4 = (bf16[2048,128]{1,0:T(8,128)(2,1)S(1)}, bf16[2048,128]{1,0:T(8,128)(2,1)S(1)}, u32[]{:S(2)}, u32[]{:S(2)}) collective-permute-start(bf16[2048,128]{1,0:T(8,128)(2,1)S(1)} %maximum_select_fusion.3), channel_id=1, source_target_pairs={{0,16},{16,0},{32,48},{48,32},{64,80},{80,64},{96,112},{112,96},{1... | collective-permute-start | bytes 1572872 | tf_op jit(solution)/shard_map/ppermute | solution.py:93
  69.5 12.7 %collective-permute-start.5 = (bf16[4096,128]{1,0:T(8,128)(2,1)S(1)}, bf16[4096,128]{1,0:T(8,128)(2,1)}, u32[]{:S(2)}, u32[]{:S(2)}) collective-permute-start(bf16[4096,128]{1,0:T(8,128)(2,1)S(1)} %maximum_select_fusion), channel_id=1, source_target_pairs={{0,1},{1,0},{2,3},{3,2},{4,5},{5,4},{6,7},{7,6},{8,9},{9,8},{10,11... | collective-permute-start | bytes 3145736 | tf_op jit(solution)/shard_map/ppermute | solution.py:97
  82.1 1.6 copy-start.3
  82.1 1.6 copy-start.13
  82.1 2.0 copy-start.4
  83.7 0.9 copy-start.5
  83.8 1.2 copy-start.6
  88.3 48.5 %copy-start.8 = (bf16[8,4096]{1,0:T(8,128)(2,1)S(1)}, bf16[8,4096]{1,0:T(8,128)(2,1)}, u32[]{:S(2)}) copy-start(bf16[8,4096]{1,0:T(8,128)(2,1)} %param.12) | copy-start | bytes 196612
  88.3 48.6 %copy-start.10 = (f32[4096]{0:T(1024)S(1)}, f32[4096]{0:T(1024)}, u32[]{:S(2)}) copy-start(f32[4096]{0:T(1024)} %param.18) | copy-start | bytes 49156
  88.3 61.3 %copy-start.9 = (s32[8,8]{1,0:T(8,128)S(1)}, s32[8,8]{1,0:T(8,128)}, u32[]{:S(2)}) copy-start(s32[8,8]{1,0:T(8,128)} %param.21) | copy-start | bytes 772
  88.3 61.3 %copy-start.11 = (f32[8,8]{1,0:T(8,128)S(1)}, f32[8,8]{1,0:T(8,128)}, u32[]{:S(2)}) copy-start(f32[8,8]{1,0:T(8,128)} %param.22) | copy-start | bytes 772
  88.3 14.1 %collective-permute-start.6 = (bf16[8,8,4096]{2,1,0:T(8,128)(2,1)S(1)}, bf16[8,8,4096]{2,1,0:T(8,128)(2,1)S(1)}, u32[]{:S(2)}, u32[]{:S(2)}) collective-permute-start(bf16[8,8,4096]{2,1,0:T(8,128)(2,1)S(1)} %fusion.26), channel_id=1, source_target_pairs={{0,1},{1,0},{2,3},{3,2},{4,5},{5,4},{6,7},{7,6},{8,9},{9,8},{10,11... | collective-permute-start | bytes 1572872 | tf_op jit(solution)/shard_map/ppermute | solution.py:152
  136.9 39.7 %copy-start.7 = (bf16[8,4096]{1,0:T(8,128)(2,1)}, bf16[8,4096]{1,0:T(8,128)(2,1)S(1)}, u32[]{:S(2)}) copy-start(bf16[8,4096]{1,0:T(8,128)(2,1)S(1)} %get-tuple-element.9) | copy-start | bytes 196612
  137.0 8.9 %collective-permute-start.8 = (bf16[8,4096]{1,0:T(8,128)(2,1)S(1)}, bf16[8,4096]{1,0:T(8,128)(2,1)S(1)}, u32[]{:S(2)}, u32[]{:S(2)}) collective-permute-start(bf16[8,4096]{1,0:T(8,128)(2,1)S(1)} %fusion.44), channel_id=1, source_target_pairs={{0,8},{2,10},{4,12},{6,14},{8,0},{10,2},{12,4},{14,6},{1,9},{3,11}... | collective-permute-start | bytes 196616 | tf_op jit(solution)/shard_map/ppermute | solution.py:174
  146.0 15.0 %collective-permute-start.9 = (bf16[16,4096]{1,0:T(8,128)(2,1)S(1)}, bf16[16,4096]{1,0:T(8,128)(2,1)S(1)}, u32[]{:S(2)}, u32[]{:S(2)}) collective-permute-start(bf16[16,4096]{1,0:T(8,128)(2,1)S(1)} %maximum_select_fusion.8), channel_id=1, source_target_pairs={{0,4},{2,6},{4,0},{6,2},{8,12},{10,14},{12,8},{14,10},{1,5},{3,7},... | collective-permute-start | bytes 393224 | tf_op jit(solution)/shard_map/ppermute | solution.py:174
  150.4 20.3 %all-to-all-start.1 = ((f32[16,1,128]{2,1,0:T(1,128)}), f32[16,1,128]{2,1,0:T(1,128)S(1)}, u32[]{:S(2)}, u32[]{:S(2)}) async-start(f32[16,1,128]{2,1,0:T(1,128)} %reshape.398), calls=%async_computation.1 | async-start | bytes 16384 | tf_op jit(solution)/shard_map/all_to_all | solution.py:162
  161.0 11.1 %collective-permute-start.10 = (bf16[32,4096]{1,0:T(8,128)(2,1)S(1)}, bf16[32,4096]{1,0:T(8,128)(2,1)S(1)}, u32[]{:S(2)}, u32[]{:S(2)}) collective-permute-start(bf16[32,4096]{1,0:T(8,128)(2,1)S(1)} %maximum_select_fusion.6), channel_id=1, source_target_pairs={{0,2},{2,0},{4,6},{6,4},{8,10},{10,8},{12,14},{14,12},{1,3},{3,1},... | collective-permute-start | bytes 786440 | tf_op jit(solution)/shard_map/ppermute | solution.py:174
  172.3 4.1 %collective-permute-start.11 = (bf16[64,4096]{1,0:T(8,128)(2,1)S(1)}, bf16[64,4096]{1,0:T(8,128)(2,1)S(1)}, u32[]{:S(2)}, u32[]{:S(2)}) collective-permute-start(bf16[64,4096]{1,0:T(8,128)(2,1)S(1)} %maximum_select_fusion.4), channel_id=1, source_target_pairs={{0,1},{1,0},{2,3},{3,2},{4,5},{5,4},{6,7},{7,6},{8,9},{9,8},{10,11... | collective-permute-start | bytes 1572872 | tf_op jit(solution)/shard_map/ppermute | solution.py:178
  205.6 25.3 %all-to-all-start.2 = ((bf16[16,8,768]{2,1,0:T(8,128)(2,1)}), bf16[16,8,768]{2,1,0:T(8,128)(2,1)S(1)}, u32[]{:S(2)}, u32[]{:S(2)}) async-start(bf16[16,8,768]{2,1,0:T(8,128)(2,1)} %bitcast.50), calls=%async_computation.2 | async-start | bytes 393216 | tf_op jit(solution)/shard_map/all_to_all | solution.py:210
Sparse Core Ops, SparseCore 0:
  82.2 115.8 all-gather.1
where the time goes:
time: 240 us; the launch traced here: 239 us
  starting transfers between devices  98.8 us (41%)
  waiting for transfers between devices  62.1 us (26%)
  blocking collectives  34 us (14%)
  other arithmetic  15.4 us (6%)
  between operations  14.8 us (6%)
  matrix products  10.1 us (4%)
  local copies, waits for them, and re-layouts  3.99 us (2%)
    all_to_all x1, blocking collectives, shards(): lax.all_to_all(pair_sum, 'zl', split_axis=0, concat_axis=0, tiled=True)  34 us
    all_gather x1, waiting for transfers between devices, shards(): w_all = lax.all_gather(w_pair, ('x', 'y'), axis=0, tiled=True)  20.8 us
    ppermute x1, starting transfers between devices, shards(): lax.ppermute(kv_local, CTX, [(i, i ^ first) for i in range(n_ctx)])  16.3 us
    ppermute x4, starting transfers between devices, shards(): other = lax.ppermute(cur, CTX, [(i, i ^ bit) for i in range(n_ctx)])  14.9 us
    all_to_all x1, waiting for transfers between devices, shards(): lax.all_to_all(hidden, EXP, split_axis=0, concat_axis=0, tiled=True)  14.1 us
    ppermute x4, waiting for transfers between devices, shards(): other = lax.ppermute(cur, CTX, [(i, i ^ bit) for i in range(n_ctx)])  12.8 us
    ppermute x1, starting transfers between devices, shards(): got = lax.ppermute(give, 'c', [(0, 1), (1, 0)])  12.6 us
    ppermute x1, starting transfers between devices, shards(): w_other = lax.ppermute(w_local, 'zh', [(0, 1), (1, 0)])  12.5 us
  transfers between devices with their start and end apart: 15, of which 10 were waited for; matrix products, arithmetic and copies ran while one was open for 8% of the time, Pallas kernels for 0%

commit v1 on v0

--- a/solution.py
+++ b/solution.py
@@ -83,7 +83,9 @@
     w_pair = jnp.where(
         zh_index == 0, jnp.concatenate([w_local, w_other]), jnp.concatenate([w_other, w_local])
     )
-    w_all = lax.all_gather(w_pair, ("x", "y"), axis=0, tiled=True)
+    w_all = jnp.concatenate(
+        lax.all_to_all(jnp.stack([w_pair] * lax.axis_size(("x", "y"))), ("x", "y"), 0, 0), axis=0
+    )
     low = ctx_index & first == 0
     cur = jnp.where(
         low, jnp.concatenate([kv_local, kv_other]), jnp.concatenate([kv_other, kv_local])

time: 240 us -> 454 us (1.89)
  waiting for transfers between devices: 62.1 us -> 290 us
  blocking collectives: 34 us -> 0 us
  starting transfers between devices: 98.8 us -> 128 us
  between operations: 14.8 us -> 1.39 us
  local copies, waits for them, and re-layouts: 3.99 us -> 9.85 us
    all_to_all x0 -> x2, waiting for transfers between devices: none -> 249 us  [the longest x1 217 us: shards(): lax.all_to_all(jnp.stack([w_pair] * lax.axis_size(('x', 'y'))), ('x', 'y'...]
    all_to_all x1 -> x0, blocking collectives: 34 us -> none  [shards(): lax.all_to_all(pair_sum, 'zl', split_axis=0, concat_axis=0, tiled=True)]
    all_gather x1 -> x0, waiting for transfers between devices: 20.8 us -> none  [shards(): w_all = lax.all_gather(w_pair, ('x', 'y'), axis=0, tiled=True)]
    all_to_all x1, starting transfers between devices: 10.6 us -> 24.9 us  [shards(): lax.all_to_all(jnp.broadcast_to(ids_rw[None], (n_exp,) + ids_rw.shape), E...]
    all_to_all x0 -> x2, starting transfers between devices: none -> 14.2 us  [the longest x1 7.36 us: shards(): lax.all_to_all(pair_sum, 'zl', split_axis=0, concat_axis=0, tiled=True)]
    ppermute x1, starting transfers between devices: 12.6 us -> 2.4 us  [shards(): got = lax.ppermute(give, 'c', [(0, 1), (1, 0)])]
    ppermute x3, starting transfers between devices: 11.5 us -> 19.9 us  [shards(): other = lax.ppermute(cur, 'zl', [(i, i ^ bit) for i in range(n_zl)])]
    another operation x0 -> x1, local copies, waits for them, and re-layouts: none -> 6.06 us  [shards(): jnp.stack([w_pair] * lax.axis_size(('x', 'y')))]
  transfers between devices with their start and end apart: 15 -> 16, of which waited for: 10 -> 13; matrix products, arithmetic and copies ran while one was open for 8% -> 4% of each run, Pallas kernels for 0% -> 0%
where the time goes in v1:
time: 454 us; the launch traced here: 453 us
  waiting for transfers between devices  290 us (64%)
  starting transfers between devices  128 us (28%)
  other arithmetic  12.5 us (3%)
  matrix products  10.1 us (2%)
  local copies, waits for them, and re-layouts  9.85 us (2%)
    all_to_all x1, waiting for transfers between devices, shards(): lax.all_to_all(jnp.stack([w_pair] * lax.axis_size(('x', 'y'))), ('x', 'y'...  217 us
    all_to_all x1, waiting for transfers between devices, shards(): lax.all_to_all(pair_sum, 'zl', split_axis=0, concat_axis=0, tiled=True)  32.7 us
    all_to_all x1, starting transfers between devices, shards(): lax.all_to_all(jnp.broadcast_to(ids_rw[None], (n_exp,) + ids_rw.shape), E...  24.9 us
    ppermute x3, starting transfers between devices, shards(): other = lax.ppermute(cur, 'zl', [(i, i ^ bit) for i in range(n_zl)])  19.9 us
    ppermute x1, starting transfers between devices, shards(): lax.ppermute(kv_local, CTX, [(i, i ^ first) for i in range(n_ctx)])  16.3 us
    ppermute x4, starting transfers between devices, shards(): other = lax.ppermute(cur, CTX, [(i, i ^ bit) for i in range(n_ctx)])  15.8 us
    ppermute x4, waiting for transfers between devices, shards(): other = lax.ppermute(cur, CTX, [(i, i ^ bit) for i in range(n_ctx)])  14.8 us
    ppermute x2, starting transfers between devices, shards(): partner = lax.ppermute(cur, 'c', [(0, 1), (1, 0)])  14.3 us
  transfers between devices with their start and end apart: 16, of which 13 were waited for; matrix products, arithmetic and copies ran while one was open for 4% of the time, Pallas kernels for 0%

profile of v1, /device:TPU:1, one launch (start us, length us, event | category | flops | bytes accessed | tf_op | source)
XLA Modules:
  0.0 452.5 jit_solution(1621672449711888879)
XLA Ops:
  0.7 0.9 dynamic-slice_select_fusion
  1.6 16.3 %collective-permute-start = (bf16[128,128]{1,0:T(8,128)(2,1)S(1)}, bf16[128,128]{1,0:T(8,128)(2,1)S(1)}, u32[]{:S(2)}, u32[]{:S(2)}) collective-permute-start(bf16[128,128]{1,0:T(8,128)(2,1)S(1)} %dynamic-slice_select_fusion), channel_id=1, source_target_pairs={{0,256},{16,272},{32,288},{48,304},{64,320},{80,336},{96,352},{112... | collective-permute-start | bytes 98312 | tf_op jit(solution)/shard_map/ppermute | solution.py:81
  17.9 1.4 collective-permute-done
  19.3 4.7 %collective-permute-start.1 = (bf16[256,128]{1,0:T(8,128)(2,1)S(1)}, bf16[256,128]{1,0:T(8,128)(2,1)S(1)}, u32[]{:S(2)}, u32[]{:S(2)}) collective-permute-start(bf16[256,128]{1,0:T(8,128)(2,1)S(1)} %maximum_select_fusion.9), channel_id=1, source_target_pairs={{0,128},{16,144},{32,160},{48,176},{64,192},{80,208},{96,224},{112... | collective-permute-start | bytes 196616 | tf_op jit(solution)/shard_map/ppermute | solution.py:95
  24.0 1.8 collective-permute-done.1
  25.9 3.1 collective-permute-start.2
  29.0 2.6 collective-permute-done.2
  31.7 4.8 %collective-permute-start.3 = (bf16[1024,128]{1,0:T(8,128)(2,1)S(1)}, bf16[1024,128]{1,0:T(8,128)(2,1)S(1)}, u32[]{:S(2)}, u32[]{:S(2)}) collective-permute-start(bf16[1024,128]{1,0:T(8,128)(2,1)S(1)} %maximum_select_fusion.5), channel_id=1, source_target_pairs={{0,32},{16,48},{32,0},{48,16},{64,96},{80,112},{96,64},{112,80},{1... | collective-permute-start | bytes 786440 | tf_op jit(solution)/shard_map/ppermute | solution.py:95
  36.5 3.8 collective-permute-done.3
  40.4 3.2 collective-permute-start.4
  43.8 6.6 %collective-permute-done.4 = bf16[2048,128]{1,0:T(8,128)(2,1)S(1)} collective-permute-done((bf16[2048,128]{1,0:T(8,128)(2,1)S(1)}, bf16[2048,128]{1,0:T(8,128)(2,1)S(1)}, u32[]{:S(2)}, u32[]{:S(2)}) %collective-permute-start.4) | collective-permute-done | bytes 524320 | tf_op jit(solution)/shard_map/ppermute | solution.py:95
  50.7 10.1 %collective-permute-start.5 = (bf16[4096,128]{1,0:T(8,128)(2,1)S(1)}, bf16[4096,128]{1,0:T(8,128)(2,1)S(1)}, u32[]{:S(2)}, u32[]{:S(2)}) collective-permute-start(bf16[4096,128]{1,0:T(8,128)(2,1)S(1)} %maximum_select_fusion), channel_id=1, source_target_pairs={{0,1},{1,0},{2,3},{3,2},{4,5},{5,4},{6,7},{7,6},{8,9},{9,8},{10,11... | collective-permute-start | bytes 3145736 | tf_op jit(solution)/shard_map/ppermute | solution.py:99
  61.2 0.8 broadcast_compare_fusion.1
  62.0 1.1 collective-permute-done.5
  64.7 0.4 fusion.20
  65.1 0.4 fusion.16
  67.1 0.5 convolution_convert_fusion.1
  67.7 2.4 collective-permute-start.6
  70.1 1.5 collective-permute-done.6
  71.6 1.0 fusion.15
  72.6 7.4 %all-to-all-start = ((bf16[8,8,4096]{2,1,0:T(8,128)(2,1)}), bf16[8,8,4096]{2,1,0:T(8,128)(2,1)S(1)}, u32[]{:S(2)}, u32[]{:S(2)}) async-start(bf16[8,8,4096]{2,1,0:T(8,128)(2,1)} %fusion.15), calls=%async_computation | async-start | bytes 1048576 | tf_op jit(solution)/shard_map/all_to_all | solution.py:157
  80.0 8.2 %collective-permute-start.7 = (bf16[48,4096]{1,0:T(8,128)(2,1)S(1)}, bf16[48,4096]{1,0:T(8,128)(2,1)}, u32[]{:S(2)}, u32[]{:S(2)}) collective-permute-start(bf16[48,4096]{1,0:T(8,128)(2,1)S(1)} %pad_maximum_fusion), channel_id=1, source_target_pairs={{0,256},{256,0},{1,257},{257,1},{2,258},{258,2},{3,259},{259,3},{4... | collective-permute-start | bytes 1179656 | tf_op jit(solution)/shard_map/ppermute | solution.py:82
  88.3 0.7 reshape.418
  89.0 32.7 %all-to-all-done = bf16[8,8,4096]{2,1,0:T(8,128)(2,1)S(1)} async-done(((bf16[8,8,4096]{2,1,0:T(8,128)(2,1)}), bf16[8,8,4096]{2,1,0:T(8,128)(2,1)S(1)}, u32[]{:S(2)}, u32[]{:S(2)}) %all-to-all-start) | async-done | bytes 524320 | tf_op jit(solution)/shard_map/all_to_all | solution.py:157
  121.7 24.9 %all-to-all-start.2 = ((f32[16,1,128]{2,1,0:T(1,128)}), f32[16,1,128]{2,1,0:T(1,128)S(1)}, u32[]{:S(2)}, u32[]{:S(2)}) async-start(f32[16,1,128]{2,1,0:T(1,128)} %reshape.418), calls=%async_computation.2 | async-start | bytes 16384 | tf_op jit(solution)/shard_map/all_to_all | solution.py:164
  146.9 0.8 fusion.47
  147.7 7.2 %collective-permute-start.8 = (bf16[8,4096]{1,0:T(8,128)(2,1)S(1)}, bf16[8,4096]{1,0:T(8,128)(2,1)S(1)}, u32[]{:S(2)}, u32[]{:S(2)}) collective-permute-start(bf16[8,4096]{1,0:T(8,128)(2,1)S(1)} %fusion.47), channel_id=1, source_target_pairs={{0,8},{2,10},{4,12},{6,14},{8,0},{10,2},{12,4},{14,6},{1,9},{3,11}... | collective-permute-start | bytes 196616 | tf_op jit(solution)/shard_map/ppermute | solution.py:176
  155.2 1.2 all-to-all-done.2
  156.4 0.5 broadcast.433
  156.9 0.7 reduce
  157.7 5.9 %collective-permute-start.9 = (bf16[16,4096]{1,0:T(8,128)(2,1)S(1)}, bf16[16,4096]{1,0:T(8,128)(2,1)S(1)}, u32[]{:S(2)}, u32[]{:S(2)}) collective-permute-start(bf16[16,4096]{1,0:T(8,128)(2,1)S(1)} %maximum_select_fusion.8), channel_id=1, source_target_pairs={{0,4},{2,6},{4,0},{6,2},{8,12},{10,14},{12,8},{14,10},{1,5},{3,7},... | collective-permute-start | bytes 393224 | tf_op jit(solution)/shard_map/ppermute | solution.py:176
  163.9 2.2 collective-permute-done.9
  166.1 6.7 %collective-permute-start.10 = (bf16[32,4096]{1,0:T(8,128)(2,1)S(1)}, bf16[32,4096]{1,0:T(8,128)(2,1)}, u32[]{:S(2)}, u32[]{:S(2)}) collective-permute-start(bf16[32,4096]{1,0:T(8,128)(2,1)S(1)} %maximum_select_fusion.6), channel_id=1, source_target_pairs={{0,2},{2,0},{4,6},{6,4},{8,10},{10,8},{12,14},{14,12},{1,3},{3,1},... | collective-permute-start | bytes 786440 | tf_op jit(solution)/shard_map/ppermute | solution.py:176
  173.2 4.7 %collective-permute-done.10 = bf16[32,4096]{1,0:T(8,128)(2,1)} collective-permute-done((bf16[32,4096]{1,0:T(8,128)(2,1)S(1)}, bf16[32,4096]{1,0:T(8,128)(2,1)}, u32[]{:S(2)}, u32[]{:S(2)}) %collective-permute-start.10) | collective-permute-done | bytes 262176 | tf_op jit(solution)/shard_map/ppermute | solution.py:176
  178.0 1.1 maximum_select_fusion.4
  179.1 4.1 collective-permute-start.11
  183.3 1.6 maximum_select_fusion.2
  184.9 6.1 %stack.2 = bf16[16,96,4096]{2,1,0:T(8,128)(2,1)} broadcast(bf16[96,4096]{1,0:T(8,128)(2,1)S(1)} %maximum_select_fusion.2), dimensions={1,2} | broadcast | bytes 13369344 | tf_op jit(solution)/shard_map/stack | solution.py:87
  191.0 6.8 %all-to-all-start.1 = ((bf16[16,96,4096]{2,1,0:T(8,128)(2,1)}), bf16[16,96,4096]{2,1,0:T(8,128)(2,1)}, u32[]{:S(2)}, u32[]{:S(2)}) async-start(bf16[16,96,4096]{2,1,0:T(8,128)(2,1)} %stack.2), calls=%async_computation.1 | async-start | bytes 25165824 | tf_op jit(solution)/shard_map/all_to_all | solution.py:87
  197.9 1.5 maximum_select_fusion.1
  199.6 0.4 convolution_convert_fusion
  200.0 216.5 %all-to-all-done.1 = bf16[16,96,4096]{2,1,0:T(8,128)(2,1)} async-done(((bf16[16,96,4096]{2,1,0:T(8,128)(2,1)}), bf16[16,96,4096]{2,1,0:T(8,128)(2,1)}, u32[]{:S(2)}, u32[]{:S(2)}) %all-to-all-start.1) | async-done | bytes 12582944 | tf_op jit(solution)/shard_map/all_to_all | solution.py:87
  416.5 6.4 %fusion.13 = f32[16,2,2,24,128]{4,3,2,1,0:T(8,128)S(1)} fusion(bf16[16,2,2,24,4096]{4,3,2,1,0:T(8,128)(2,1)} %bitcast.43, bf16[128,4096]{1,0:T(8,128)(2,1)S(1)} %convolution_convert_fusion), kind=kOutput, calls=%fused_computation.26 | convolution fusion | flops 1610612736 | bytes 14417920 | tf_op jit(solution)/shard_map/fd,sd->fs/dot_general | solution.py:207
  423.1 0.8 copy.132
  424.0 12.5 %all-to-all-start.3 = ((bf16[16,8,768]{2,1,0:T(8,128)(2,1)}), bf16[16,8,768]{2,1,0:T(8,128)(2,1)S(1)}, u32[]{:S(2)}, u32[]{:S(2)}) async-start(bf16[16,8,768]{2,1,0:T(8,128)(2,1)} %bitcast.52), calls=%async_computation.3 | async-start | bytes 393216 | tf_op jit(solution)/shard_map/all_to_all | solution.py:212
  437.0 14.1 %all-to-all-done.3 = bf16[16,8,768]{2,1,0:T(8,128)(2,1)S(1)} async-done(((bf16[16,8,768]{2,1,0:T(8,128)(2,1)}), bf16[16,8,768]{2,1,0:T(8,128)(2,1)S(1)}, u32[]{:S(2)}, u32[]{:S(2)}) %all-to-all-start.3) | async-done | bytes 196640 | tf_op jit(solution)/shard_map/all_to_all | solution.py:212
  451.1 0.7 gather_fusion
  451.8 0.7 bitcast_select_fusion.2
  (99 shorter events, 6.4 us)
Async XLA Ops:
  0.6 66.5 %copy-start = (bf16[256,4096]{1,0:T(8,128)(2,1)S(1)}, bf16[256,4096]{1,0:T(8,128)(2,1)}, u32[]{:S(2)}) copy-start(bf16[256,4096]{1,0:T(8,128)(2,1)} %param.17) | copy-start | bytes 6291460
  0.6 43.1 %copy-start.8 = (s32[32]{0:T(128)S(1)}, s32[32]{0:T(128)}, u32[]{:S(2)}) copy-start(s32[32]{0:T(128)} %constant.185) | copy-start | bytes 388
  0.7 43.0 %copy-start.7 = (s32[64]{0:T(128)S(1)}, s32[64]{0:T(128)}, u32[]{:S(2)}) copy-start(s32[64]{0:T(128)} %param.16) | copy-start | bytes 772
  1.6 17.7 %collective-permute-start = (bf16[128,128]{1,0:T(8,128)(2,1)S(1)}, bf16[128,128]{1,0:T(8,128)(2,1)S(1)}, u32[]{:S(2)}, u32[]{:S(2)}) collective-permute-start(bf16[128,128]{1,0:T(8,128)(2,1)S(1)} %dynamic-slice_select_fusion), channel_id=1, source_target_pairs={{0,256},{16,272},{32,288},{48,304},{64,320},{80,336},{96,352},{112... | collective-permute-start | bytes 98312 | tf_op jit(solution)/shard_map/ppermute | solution.py:81
  19.3 6.5 %collective-permute-start.1 = (bf16[256,128]{1,0:T(8,128)(2,1)S(1)}, bf16[256,128]{1,0:T(8,128)(2,1)S(1)}, u32[]{:S(2)}, u32[]{:S(2)}) collective-permute-start(bf16[256,128]{1,0:T(8,128)(2,1)S(1)} %maximum_select_fusion.9), channel_id=1, source_target_pairs={{0,128},{16,144},{32,160},{48,176},{64,192},{80,208},{96,224},{112... | collective-permute-start | bytes 196616 | tf_op jit(solution)/shard_map/ppermute | solution.py:95
  25.9 5.7 %collective-permute-start.2 = (bf16[512,128]{1,0:T(8,128)(2,1)S(1)}, bf16[512,128]{1,0:T(8,128)(2,1)S(1)}, u32[]{:S(2)}, u32[]{:S(2)}) collective-permute-start(bf16[512,128]{1,0:T(8,128)(2,1)S(1)} %maximum_select_fusion.7), channel_id=1, source_target_pairs={{0,64},{16,80},{32,96},{48,112},{64,0},{80,16},{96,32},{112,48},{1... | collective-permute-start | bytes 393224 | tf_op jit(solution)/shard_map/ppermute | solution.py:95
  31.7 8.6 %collective-permute-start.3 = (bf16[1024,128]{1,0:T(8,128)(2,1)S(1)}, bf16[1024,128]{1,0:T(8,128)(2,1)S(1)}, u32[]{:S(2)}, u32[]{:S(2)}) collective-permute-start(bf16[1024,128]{1,0:T(8,128)(2,1)S(1)} %maximum_select_fusion.5), channel_id=1, source_target_pairs={{0,32},{16,48},{32,0},{48,16},{64,96},{80,112},{96,64},{112,80},{1... | collective-permute-start | bytes 786440 | tf_op jit(solution)/shard_map/ppermute | solution.py:95
  40.4 10.0 %collective-permute-start.4 = (bf16[2048,128]{1,0:T(8,128)(2,1)S(1)}, bf16[2048,128]{1,0:T(8,128)(2,1)S(1)}, u32[]{:S(2)}, u32[]{:S(2)}) collective-permute-start(bf16[2048,128]{1,0:T(8,128)(2,1)S(1)} %maximum_select_fusion.3), channel_id=1, source_target_pairs={{0,16},{16,0},{32,48},{48,32},{64,80},{80,64},{96,112},{112,96},{1... | collective-permute-start | bytes 1572872 | tf_op jit(solution)/shard_map/ppermute | solution.py:95
  50.7 12.4 %collective-permute-start.5 = (bf16[4096,128]{1,0:T(8,128)(2,1)S(1)}, bf16[4096,128]{1,0:T(8,128)(2,1)S(1)}, u32[]{:S(2)}, u32[]{:S(2)}) collective-permute-start(bf16[4096,128]{1,0:T(8,128)(2,1)S(1)} %maximum_select_fusion), channel_id=1, source_target_pairs={{0,1},{1,0},{2,3},{3,2},{4,5},{5,4},{6,7},{7,6},{8,9},{9,8},{10,11... | collective-permute-start | bytes 3145736 | tf_op jit(solution)/shard_map/ppermute | solution.py:99
  62.0 1.3 copy-start.9
  67.6 12.4 %copy-start.1 = (bf16[1,4096,24]{1,2,0:T(8,128)(2,1)S(1)}, bf16[1,4096,24]{1,2,0:T(8,128)(2,1)}, u32[]{:S(2)}) copy-start(bf16[1,4096,24]{1,2,0:T(8,128)(2,1)} %param.20) | copy-start | bytes 589828
  67.6 12.4 %copy-start.2 = (bf16[1,4096,24]{1,2,0:T(8,128)(2,1)S(1)}, bf16[1,4096,24]{1,2,0:T(8,128)(2,1)}, u32[]{:S(2)}) copy-start(bf16[1,4096,24]{1,2,0:T(8,128)(2,1)} %param.19) | copy-start | bytes 589828
  67.7 20.5 %copy-start.5 = (s32[8,8]{1,0:T(8,128)S(1)}, s32[8,8]{1,0:T(8,128)}, u32[]{:S(2)}) copy-start(s32[8,8]{1,0:T(8,128)} %param.21) | copy-start | bytes 772
  67.7 20.5 %copy-start.6 = (f32[8,8]{1,0:T(8,128)S(1)}, f32[8,8]{1,0:T(8,128)}, u32[]{:S(2)}) copy-start(f32[8,8]{1,0:T(8,128)} %param.22) | copy-start | bytes 772
  67.7 79.0 %copy-start.4 = (bf16[8,4096]{1,0:T(8,128)(2,1)S(1)}, bf16[8,4096]{1,0:T(8,128)(2,1)}, u32[]{:S(2)}) copy-start(bf16[8,4096]{1,0:T(8,128)(2,1)} %param.12) | copy-start | bytes 196612
  67.7 3.9 collective-permute-start.6
  72.6 49.1 %all-to-all-start = ((bf16[8,8,4096]{2,1,0:T(8,128)(2,1)}), bf16[8,8,4096]{2,1,0:T(8,128)(2,1)S(1)}, u32[]{:S(2)}, u32[]{:S(2)}) async-start(bf16[8,8,4096]{2,1,0:T(8,128)(2,1)} %fusion.15), calls=%async_computation | async-start | bytes 1048576 | tf_op jit(solution)/shard_map/all_to_all | solution.py:157
  80.0 103.3 %collective-permute-start.7 = (bf16[48,4096]{1,0:T(8,128)(2,1)S(1)}, bf16[48,4096]{1,0:T(8,128)(2,1)}, u32[]{:S(2)}, u32[]{:S(2)}) collective-permute-start(bf16[48,4096]{1,0:T(8,128)(2,1)S(1)} %pad_maximum_fusion), channel_id=1, source_target_pairs={{0,256},{256,0},{1,257},{257,1},{2,258},{258,2},{3,259},{259,3},{4... | collective-permute-start | bytes 1179656 | tf_op jit(solution)/shard_map/ppermute | solution.py:82
  121.7 34.7 %all-to-all-start.2 = ((f32[16,1,128]{2,1,0:T(1,128)}), f32[16,1,128]{2,1,0:T(1,128)S(1)}, u32[]{:S(2)}, u32[]{:S(2)}) async-start(f32[16,1,128]{2,1,0:T(1,128)} %reshape.418), calls=%async_computation.2 | async-start | bytes 16384 | tf_op jit(solution)/shard_map/all_to_all | solution.py:164
  146.9 44.2 %copy-start.3 = (bf16[8,4096]{1,0:T(8,128)(2,1)}, bf16[8,4096]{1,0:T(8,128)(2,1)S(1)}, u32[]{:S(2)}) copy-start(bf16[8,4096]{1,0:T(8,128)(2,1)S(1)} %get-tuple-element.9) | copy-start | bytes 196612
  147.7 10.0 %collective-permute-start.8 = (bf16[8,4096]{1,0:T(8,128)(2,1)S(1)}, bf16[8,4096]{1,0:T(8,128)(2,1)S(1)}, u32[]{:S(2)}, u32[]{:S(2)}) collective-permute-start(bf16[8,4096]{1,0:T(8,128)(2,1)S(1)} %fusion.47), channel_id=1, source_target_pairs={{0,8},{2,10},{4,12},{6,14},{8,0},{10,2},{12,4},{14,6},{1,9},{3,11}... | collective-permute-start | bytes 196616 | tf_op jit(solution)/shard_map/ppermute | solution.py:176
  157.7 8.3 %collective-permute-start.9 = (bf16[16,4096]{1,0:T(8,128)(2,1)S(1)}, bf16[16,4096]{1,0:T(8,128)(2,1)S(1)}, u32[]{:S(2)}, u32[]{:S(2)}) collective-permute-start(bf16[16,4096]{1,0:T(8,128)(2,1)S(1)} %maximum_select_fusion.8), channel_id=1, source_target_pairs={{0,4},{2,6},{4,0},{6,2},{8,12},{10,14},{12,8},{14,10},{1,5},{3,7},... | collective-permute-start | bytes 393224 | tf_op jit(solution)/shard_map/ppermute | solution.py:176
  166.1 11.9 %collective-permute-start.10 = (bf16[32,4096]{1,0:T(8,128)(2,1)S(1)}, bf16[32,4096]{1,0:T(8,128)(2,1)}, u32[]{:S(2)}, u32[]{:S(2)}) collective-permute-start(bf16[32,4096]{1,0:T(8,128)(2,1)S(1)} %maximum_select_fusion.6), channel_id=1, source_target_pairs={{0,2},{2,0},{4,6},{6,4},{8,10},{10,8},{12,14},{14,12},{1,3},{3,1},... | collective-permute-start | bytes 786440 | tf_op jit(solution)/shard_map/ppermute | solution.py:176
  179.1 18.8 %collective-permute-start.11 = (bf16[64,4096]{1,0:T(8,128)(2,1)S(1)}, bf16[64,4096]{1,0:T(8,128)(2,1)}, u32[]{:S(2)}, u32[]{:S(2)}) collective-permute-start(bf16[64,4096]{1,0:T(8,128)(2,1)S(1)} %maximum_select_fusion.4), channel_id=1, source_target_pairs={{0,1},{1,0},{2,3},{3,2},{4,5},{5,4},{6,7},{7,6},{8,9},{9,8},{10,11... | collective-permute-start | bytes 1572872 | tf_op jit(solution)/shard_map/ppermute | solution.py:180
  191.0 225.5 %all-to-all-start.1 = ((bf16[16,96,4096]{2,1,0:T(8,128)(2,1)}), bf16[16,96,4096]{2,1,0:T(8,128)(2,1)}, u32[]{:S(2)}, u32[]{:S(2)}) async-start(bf16[16,96,4096]{2,1,0:T(8,128)(2,1)} %stack.2), calls=%async_computation.1 | async-start | bytes 25165824 | tf_op jit(solution)/shard_map/all_to_all | solution.py:87
  424.0 27.1 %all-to-all-start.3 = ((bf16[16,8,768]{2,1,0:T(8,128)(2,1)}), bf16[16,8,768]{2,1,0:T(8,128)(2,1)S(1)}, u32[]{:S(2)}, u32[]{:S(2)}) async-start(bf16[16,8,768]{2,1,0:T(8,128)(2,1)} %bitcast.52), calls=%async_computation.3 | async-start | bytes 393216 | tf_op jit(solution)/shard_map/all_to_all | solution.py:212
